TPU v7x, 32 devices: a whole 2x2x4 slice. The times are simulated.
32 devices in a mesh: groups: 2 (over x), tm: 16 (over z, y, core).
Axes of the slice: x: 2, y: 2, z: 4, core: 2. Of those that a mesh axis runs over, the one named last changes fastest.
Arguments:
- observed: float32 [32, 128], P(('groups', 'tm')), parts along dimension 0, may hold values from -6 to 6
- obs_masks: int32 [32, 128], P(('groups', 'tm')), parts along dimension 0, may hold values 0 or 1
- decay_rates: float32 [256], P('groups'), parts along dimension 0, may hold values from 0.05 to 0.5
- noise_var: float32 [256], P('groups'), parts along dimension 0, may hold values from 0.05 to 0.5
- spatial_cov: float32 [256, 128], P('groups'), parts along dimension 0, may hold values from -1 to 4, as said below
Outputs:
- smooth_mean: float32 [32, 256], P(('groups', 'tm')), parts along dimension 0
- smooth_cov: float32 [32, 256, 256], P(('groups', 'tm')), parts along dimension 0
There are 2 independent parts, one for each index of `groups`. A program takes and returns all parts, laid end to end along the dimension named above; each array names one. Nothing has to cross between parts.
Inputs may be any that keep to these rules, and one draw needn't show every extreme that they name: spatial_cov is symmetric, and each diagonal entry is positive and larger than the sum of the magnitudes of the other entries of its row.
All inputs are finite; a program needn't handle non-finite values. No bound on the sum of `obs_masks` on one device may be relied on, other than what follows from the above.
Results may differ from a plain program's by a relative error of at most 0.0003.
Values sent between devices are 32-bit elements; how exact they have to be, the bound alone decides.
No kernel may reach another device: no remote copies, remote signals or barrier semaphores. Data moves between devices by JAX's collectives and lax.ppermute only.
A program may use at most 128 MiB of HBM per device.

v0:
```python
import jax
import jax.numpy as jnp
from jax import lax
from jax.sharding import PartitionSpec as P

HIGHEST = lax.Precision.HIGHEST
JITTER = 0.001


def matmul_hi(left, right):
    return jnp.matmul(left, right, precision=HIGHEST)


def swap_last(matrix):
    return jnp.swapaxes(matrix, -1, -2)


def apply_trans(transit, matrix):
    points = transit.shape[1]
    upper_half = matrix[..., :points, :]
    lower_half = matrix[..., points:, :]
    return jnp.concatenate(
        [
            transit[0][:, None] * upper_half + transit[1][:, None] * lower_half,
            transit[2][:, None] * upper_half + transit[3][:, None] * lower_half,
        ],
        axis=-2,
    )


def build_model(decay_rates, spatial_cov):
    decay_one = jnp.exp(-decay_rates)
    transit = jnp.stack(
        [
            decay_one * (1.0 + decay_rates),
            decay_one * decay_rates,
            -decay_one * decay_rates,
            decay_one * (1.0 - decay_rates),
        ]
    )
    decay_two = jnp.exp(-2.0 * decay_rates)
    var_ff = 1.0 - decay_two * (1.0 + 2.0 * decay_rates + 2.0 * decay_rates * decay_rates)
    cov_fg = 2.0 * decay_rates * decay_rates * decay_two
    var_gg = 1.0 - decay_two * (1.0 - 2.0 * decay_rates + 2.0 * decay_rates * decay_rates)
    fac_ff = jnp.sqrt(var_ff)
    fac_gf = cov_fg / fac_ff
    fac_gg = jnp.sqrt(var_gg - fac_gf * fac_gf)

    def scaled(left, right):
        return left[:, None] * spatial_cov * right[None, :]

    zero_block = jnp.zeros_like(spatial_cov)
    process = jnp.block(
        [
            [scaled(fac_ff, fac_ff), scaled(fac_ff, fac_gf)],
            [scaled(fac_gf, fac_ff), scaled(fac_gf, fac_gf) + scaled(fac_gg, fac_gg)],
        ]
    )
    process = process + JITTER * jnp.eye(2 * spatial_cov.shape[0], dtype=jnp.float32)
    prior = jnp.block([[spatial_cov, zero_block], [zero_block, spatial_cov]])
    return (transit, process, prior)


def predict(transit, process, mean, cov):
    forward_cov = apply_trans(transit, cov)
    cov_pred = apply_trans(transit, swap_last(forward_cov)) + process
    mean_pred = apply_trans(transit, mean[:, None])[:, 0]
    return (mean_pred, cov_pred)


def kalman_update(mean_pred, cov_pred, obs, root):
    points = obs.shape[-1]
    normal = (
        jnp.eye(points, dtype=jnp.float32)
        + root[:, None] * cov_pred[:points, :points] * root[None, :]
    )
    factor = jnp.linalg.cholesky(normal)
    innovation = root * (obs - mean_pred[:points])
    rhs = jnp.concatenate([root[:, None] * cov_pred[:points, :], innovation[:, None]], axis=1)
    half = lax.linalg.triangular_solve(factor, rhs, left_side=True, lower=True)
    gain_half = half[:, :-1]
    cov_new = cov_pred - matmul_hi(swap_last(gain_half), gain_half)
    mean_new = mean_pred + matmul_hi(swap_last(gain_half), half[:, -1])
    return (mean_new, cov_new)


def smoother_elements(means, covs, last_flag, transit, process):
    forward_cov = apply_trans(transit, covs)
    predicted = apply_trans(transit, swap_last(forward_cov)) + process
    factor = jnp.linalg.cholesky(predicted)
    half_solve = lax.linalg.triangular_solve(factor, forward_cov, left_side=True, lower=True)
    gain_t = lax.linalg.triangular_solve(
        factor, half_solve, left_side=True, lower=True, transpose_a=True
    )
    gains = swap_last(gain_t) * (1.0 - last_flag.astype(jnp.float32))[:, None, None]
    forward_mean = apply_trans(transit, means[..., None])
    shift_means = means - matmul_hi(gains, forward_mean)[..., 0]
    shift_covs = covs - matmul_hi(gains, forward_cov)
    return (gains, shift_means, shift_covs)


def smooth_join(lower_el, higher_el):
    gain_a, mean_a, cov_a = lower_el
    gain_b, mean_b, cov_b = higher_el
    return (
        matmul_hi(gain_a, gain_b),
        matmul_hi(gain_a, mean_b[..., None])[..., 0] + mean_a,
        matmul_hi(matmul_hi(gain_a, cov_b), swap_last(gain_a)) + cov_a,
    )


def shards(observed, obs_masks, decay_rates, noise_var, spatial_cov):
    transit, process, prior = build_model(decay_rates, spatial_cov)
    local_steps, points = observed.shape
    width = 2 * points
    position = lax.axis_index("tm")
    tm_count = lax.axis_size("tm")
    total_steps = tm_count * local_steps
    root_local = jnp.sqrt(obs_masks.astype(jnp.float32) / noise_var)
    packed = jnp.stack([observed, root_local], axis=1)
    gathered = lax.all_gather(packed, "tm", tiled=True)
    obs_all = gathered[:, 0]
    root_all = gathered[:, 1]
    mean_first, cov_first = kalman_update(
        jnp.zeros((width,), jnp.float32), prior, obs_all[0], root_all[0]
    )
    last_local = position * local_steps + (local_steps - 1)

    def filter_step(step, mean, cov):
        mean_pred, cov_pred = predict(transit, process, mean, cov)
        obs_now = lax.dynamic_index_in_dim(obs_all, step, keepdims=False)
        root_now = lax.dynamic_index_in_dim(root_all, step, keepdims=False)
        return kalman_update(mean_pred, cov_pred, obs_now, root_now)

    if local_steps == 1:

        def body(step, carry):
            return filter_step(step, carry[0], carry[1])

        mean_last, cov_last = lax.fori_loop(1, last_local + 1, body, (mean_first, cov_first))
        means = mean_last[None]
        covs = cov_last[None]
    else:
        mean_buf = jnp.zeros((local_steps, width), jnp.float32).at[0].set(mean_first)
        cov_buf = jnp.zeros((local_steps, width, width), jnp.float32).at[0].set(cov_first)

        def body(step, carry):
            mean, cov, mean_buf, cov_buf = carry
            mean, cov = filter_step(step, mean, cov)
            slot = step % local_steps
            mean_buf = lax.dynamic_update_index_in_dim(mean_buf, mean, slot, 0)
            cov_buf = lax.dynamic_update_index_in_dim(cov_buf, cov, slot, 0)
            return (mean, cov, mean_buf, cov_buf)

        _, _, means, covs = lax.fori_loop(
            1, last_local + 1, body, (mean_first, cov_first, mean_buf, cov_buf)
        )
    global_step = position * local_steps + jnp.arange(local_steps)
    last_flag = global_step == total_steps - 1
    if local_steps == 1:

        def compute_elements(operand):
            return smoother_elements(operand[0], operand[1], last_flag, transit, process)

        def final_elements(operand):
            return (jnp.zeros_like(operand[1]), operand[0], operand[1])

        smooth = lax.cond(position == tm_count - 1, final_elements, compute_elements, (means, covs))
    else:
        smooth = smoother_elements(means, covs, last_flag, transit, process)
    if local_steps > 1:
        last_el = jax.tree.map(lambda leaf: leaf[-1], smooth)
        front_els = jax.tree.map(lambda leaf: leaf[:-1], smooth)

        def backward(running, element):
            joined = smooth_join(element, running)
            return (joined, joined)

        _, head_els = lax.scan(backward, last_el, front_els, reverse=True)
        suffixes = jax.tree.map(
            lambda head_leaf, last_leaf: jnp.concatenate([head_leaf, last_leaf[None]], axis=0),
            head_els,
            last_el,
        )
        block_total = jax.tree.map(lambda leaf: leaf[0], suffixes)
    else:
        block_total = jax.tree.map(lambda leaf: leaf[0], smooth)
    running = block_total
    shift = 1
    while shift < tm_count:
        pairs = [(source, source - shift) for source in range(shift, tm_count)]
        received = lax.ppermute(running, "tm", pairs)
        running = smooth_join(running, received)
        shift *= 2
    if local_steps == 1:
        return (running[1][None], running[2][None])
    pairs = [(source, source - 1) for source in range(1, tm_count)]
    after_mine = lax.ppermute(running, "tm", pairs)
    gains, shift_means, shift_covs = suffixes
    smooth_mean = matmul_hi(gains, after_mine[1][:, None])[..., 0] + shift_means
    smooth_cov = matmul_hi(matmul_hi(gains, after_mine[2]), swap_last(gains)) + shift_covs
    return (smooth_mean, smooth_cov)


def solution(mesh):
    placed = (
        P(("groups", "tm"), None),
        P(("groups", "tm"), None),
        P("groups"),
        P("groups"),
        P("groups", None),
    )
    return jax.shard_map(
        shards,
        mesh=mesh,
        in_specs=placed,
        out_specs=(P(("groups", "tm"), None), P(("groups", "tm"), None, None)),
        check_vma=False,
    )
```

profile of v0, /device:TPU:1, one launch (start us, length us, event | category | flops | bytes accessed | tf_op | source)
XLA Modules:
  0.0 498.3 jit_solution(2744481612989866936)
XLA Ops:
  2.0 23.1 %all_gather.3 = f32[16,2,128]{2,1,0:T(2,128)S(1)} all-gather(f32[1,2,128]{2,1,0:T(2,128)S(1)} %pad_maximum_fusion.3), channel_id=1, replica_groups=mesh['groups'=2,'tm'=16] {'tm'}, dimensions={0}, use_global_device_ids=true | all-gather | bytes 17408 | tf_op jit(solution)/shard_map/all_gather | solution.py:121
  25.7 11.7 %custom-call.32 = f32[128,128]{1,0:T(8,128)S(1)} custom-call(f32[128,128]{1,0:T(8,128)S(1)} %fusion.49), custom_call_target="Cholesky" | custom-call | tf_op jit(solution)/shard_map/jit(cholesky)/cholesky/custom-call.1 | solution.py:77
  38.8 9.8 %custom-call.33 = f32[1,128,128]{1,2,0:T(8,128)S(1)} custom-call(f32[1,128,128]{2,1,0:T(8,128)S(1)} %fusion.47), custom_call_target="InvertDiagBlocksLowerTriangular" | custom-call | tf_op jit(solution)/shard_map/triangular_solve/custom-call.0 | solution.py:80
  49.9 24.9 %while.14 = (s32[]{:T(128)}, f32[256]{0:T(256)S(1)}, f32[256,256]{0,1:T(8,128)S(1)}, s32[]{:T(128)}, f32[128]{0:T(128)S(1)}, /*index=5*/f32[128]{0:T(128)S(1)}, ...) while((s32[]{:T(128)}, f32[256]{0:T(256)S(1)}, ...), condition=%wide.region_3.6_spmd, body=%wide.region_2.5_spmd.sunk | while | flops 152618752 | bytes 5461689 | solution.py:140
  51.0 11.7 %custom-call.37 = f32[128,128]{1,0:T(8,128)S(1)} custom-call(f32[128,128]{1,0:T(8,128)S(1)} %fusion.129), custom_call_target="Cholesky" | custom-call | tf_op jit(solution)/shard_map/while/body/jit(cholesky)/cholesky/custom-call.1 | solution.py:77
  64.0 9.8 %custom-call.38 = f32[1,128,128]{1,2,0:T(8,128)S(1)} custom-call(f32[1,128,128]{2,1,0:T(8,128)S(1)} %fusion.130), custom_call_target="InvertDiagBlocksLowerTriangular" | custom-call | tf_op jit(solution)/shard_map/while/body/triangular_solve/custom-call.0 | solution.py:80
  74.9 63.7 %conditional.1 = (f32[1,256]{1,0:T(1,128)S(1)}, f32[256,256]{0,1:T(8,128)S(1)}, f32[1,256,256]{2,1,0:T(8,128)S(1)}) conditional(s32[]{:T(128)} %convert_element_type.18, (f32[128]{0:T(128)S(1)}, f32[1,256,256]{1,2,0:T(8,128)S(1)}, f32[128]{0:T(128)S(1)}, f32[128]{0:T(128)S(1)}, f32[128]{0:T(128)S(1)}, /*index=5*/f32[256,256]{0,1:T(8,128)S(1)}, ...), branch_computations={%region_4.11_spmd, %region_9.12_spmd} | conditional | flops 556025344 | bytes 11482373 | solution.py:168
  76.0 11.7 %custom-call.24 = f32[1,128,128]{2,1,0:T(8,128)S(1)} custom-call(f32[1,128,128]{2,1,0:T(8,128)S(1)} %cholesky.48), custom_call_target="Cholesky" | custom-call | tf_op jit(solution)/shard_map/cond/branch_0_fun/jit(cholesky)/cholesky | solution.py:90
  87.7 9.8 %custom-call.25 = f32[1,1,128,128]{2,3,1,0:T(8,128)S(1)} custom-call(f32[1,1,128,128]{3,2,1,0:T(8,128)S(1)} %get-tuple-element.221), custom_call_target="InvertDiagBlocksLowerTriangular" | custom-call | tf_op jit(solution)/shard_map/cond/branch_0_fun/jit(cholesky)/cholesky | solution.py:90
  98.0 11.7 %custom-call.26 = f32[1,128,128]{2,1,0:T(8,128)S(1)} custom-call(f32[1,128,128]{2,1,0:T(8,128)S(1)} %fusion.20), custom_call_target="Cholesky" | custom-call | tf_op jit(solution)/shard_map/cond/branch_0_fun/jit(cholesky)/cholesky | solution.py:90
  111.8 4.0 while.13
  112.5 1.3 bitcast_dynamic-update-slice_fusion.3
  114.4 1.3 bitcast_dynamic-update-slice_fusion.3
  115.7 19.7 %custom-call.27 = f32[1,2,128,128]{2,3,1,0:T(8,128)S(1)} custom-call(f32[1,2,128,128]{3,2,1,0:T(8,128)S(1)} %bitcast.262), custom_call_target="InvertDiagBlocksLowerTriangular" | custom-call | tf_op jit(solution)/shard_map/cond/branch_0_fun/triangular_solve | solution.py:92
  138.6 1.9 collective-permute-start.7
  140.5 1.9 collective-permute-start.3
  142.4 1.9 collective-permute-start
  144.3 22.5 %collective-permute-done.3 = f32[256]{0:T(256)S(1)} collective-permute-done((f32[256]{0:T(256)S(1)}, f32[256]{0:T(256)S(1)}, u32[]{:S(2)}, u32[]{:S(2)}) %collective-permute-start.3) | collective-permute-done | bytes 1056 | tf_op jit(solution)/shard_map/ppermute | solution.py:192
  167.0 1.3 collective-permute-start.4
  169.4 1.3 collective-permute-start.8
  171.3 1.3 collective-permute-start.1
  172.6 48.7 %collective-permute-done.4 = f32[256]{0:T(256)S(1)} collective-permute-done((f32[256]{0:T(256)S(1)}, f32[256]{0:T(256)S(1)}, u32[]{:S(2)}, u32[]{:S(2)}) %collective-permute-start.4) | collective-permute-done | bytes 1056 | tf_op jit(solution)/shard_map/ppermute | solution.py:192
  221.6 1.3 collective-permute-start.5
  222.9 4.1 collective-permute-done.8
  227.8 1.3 collective-permute-start.9
  230.2 1.3 collective-permute-start.2
  231.5 89.9 %collective-permute-done.5 = f32[256]{0:T(256)S(1)} collective-permute-done((f32[256]{0:T(256)S(1)}, f32[256]{0:T(256)S(1)}, u32[]{:S(2)}, u32[]{:S(2)}) %collective-permute-start.5) | collective-permute-done | bytes 1056 | tf_op jit(solution)/shard_map/ppermute | solution.py:192
  321.7 1.3 collective-permute-start.6
  323.1 7.4 %collective-permute-done.9 = f32[256,256]{1,0:T(8,128)S(1)} collective-permute-done((f32[256,256]{1,0:T(8,128)S(1)}, f32[256,256]{1,0:T(8,128)S(1)}, u32[]{:S(2)}, u32[]{:S(2)}) %collective-permute-start.9) | collective-permute-done | bytes 262176 | tf_op jit(solution)/shard_map/ppermute | solution.py:192
  331.3 1.3 collective-permute-start.10
  333.7 145.0 %collective-permute-done.6 = f32[256]{0:T(256)S(1)} collective-permute-done((f32[256]{0:T(256)S(1)}, f32[256]{0:T(256)S(1)}, u32[]{:S(2)}, u32[]{:S(2)}) %collective-permute-start.6) | collective-permute-done | bytes 1056 | tf_op jit(solution)/shard_map/ppermute | solution.py:192
  479.6 17.0 %collective-permute-done.10 = f32[256,256]{1,0:T(8,128)S(1)} collective-permute-done((f32[256,256]{1,0:T(8,128)S(1)}, f32[256,256]{1,0:T(8,128)S(1)}, u32[]{:S(2)}, u32[]{:S(2)}) %collective-permute-start.10) | collective-permute-done | bytes 262176 | tf_op jit(solution)/shard_map/ppermute | solution.py:192
  (107 shorter events, 21.8 us)
Async XLA Ops:
  0.6 0.7 copy-start.3
  0.6 0.7 copy-start.4
  1.3 0.7 copy-start.1
  2.0 23.2 %copy-start.2 = (f32[128]{0:T(128)S(1)}, f32[128]{0:T(128)}, u32[]{:S(2)}) copy-start(f32[128]{0:T(128)} %param.14) | copy-start | bytes 1540
  2.0 23.3 %copy-start = (f32[128,128]{1,0:T(8,128)S(1)}, f32[128,128]{1,0:T(8,128)}, u32[]{:S(2)}) copy-start(f32[128,128]{1,0:T(8,128)} %param.16) | copy-start | bytes 196612
  138.6 29.8 %collective-permute-start.7 = (f32[256,256]{1,0:T(8,128)S(1)}, f32[256,256]{1,0:T(8,128)S(1)}, u32[]{:S(2)}, u32[]{:S(2)}) collective-permute-start(f32[256,256]{1,0:T(8,128)S(1)} %bitcast.242), channel_id=1, source_target_pairs={{1,0},{2,1},{3,2},{4,3},{5,4},{6,5},{7,6},{8,7},{9,8},{10,9},{11,1... | collective-permute-start | bytes 786440 | tf_op jit(solution)/shard_map/ppermute | solution.py:192
  140.5 26.3 %collective-permute-start.3 = (f32[256]{0:T(256)S(1)}, f32[256]{0:T(256)S(1)}, u32[]{:S(2)}, u32[]{:S(2)}) collective-permute-start(f32[256]{0:T(256)S(1)} %bitcast.255), channel_id=1, source_target_pairs={{1,0},{2,1},{3,2},{4,3},{5,4},{6,5},{7,6},{8,7},{9,8},{10,9},{11,1... | collective-permute-start | bytes 3080 | tf_op jit(solution)/shard_map/ppermute | solution.py:192
  142.4 28.2 %collective-permute-start = (f32[256,256]{0,1:T(8,128)S(1)}, f32[256,256]{0,1:T(8,128)S(1)}, u32[]{:S(2)}, u32[]{:S(2)}) collective-permute-start(f32[256,256]{0,1:T(8,128)S(1)} %get-tuple-element.136), channel_id=1, source_target_pairs={{1,0},{2,1},{3,2},{4,3},{5,4},{6,5},{7,6},{8,7},{9,8},{10,9},{11,1... | collective-permute-start | bytes 786440 | tf_op jit(solution)/shard_map/ppermute | solution.py:192
  167.0 54.3 %collective-permute-start.4 = (f32[256]{0:T(256)S(1)}, f32[256]{0:T(256)S(1)}, u32[]{:S(2)}, u32[]{:S(2)}) collective-permute-start(f32[256]{0:T(256)S(1)} %add.183), channel_id=1, source_target_pairs={{2,0},{3,1},{4,2},{5,3},{6,4},{7,5},{8,6},{9,7},{10,8},{11,9},{12,... | collective-permute-start | bytes 3080 | tf_op jit(solution)/shard_map/ppermute | solution.py:192
  169.4 57.7 %collective-permute-start.8 = (f32[256,256]{1,0:T(8,128)S(1)}, f32[256,256]{1,0:T(8,128)S(1)}, u32[]{:S(2)}, u32[]{:S(2)}) collective-permute-start(f32[256,256]{1,0:T(8,128)S(1)} %convolution_add_fusion.3), channel_id=1, source_target_pairs={{2,0},{3,1},{4,2},{5,3},{6,4},{7,5},{8,6},{9,7},{10,8},{11,9},{12,... | collective-permute-start | bytes 786440 | tf_op jit(solution)/shard_map/ppermute | solution.py:192
  171.3 58.6 %collective-permute-start.1 = (f32[256,256]{1,0:T(8,128)S(1)}, f32[256,256]{1,0:T(8,128)S(1)}, u32[]{:S(2)}, u32[]{:S(2)}) collective-permute-start(f32[256,256]{1,0:T(8,128)S(1)} %fusion.59), channel_id=1, source_target_pairs={{2,0},{3,1},{4,2},{5,3},{6,4},{7,5},{8,6},{9,7},{10,8},{11,9},{12,... | collective-permute-start | bytes 786440 | tf_op jit(solution)/shard_map/ppermute | solution.py:192
  221.6 99.9 %collective-permute-start.5 = (f32[256]{0:T(256)S(1)}, f32[256]{0:T(256)S(1)}, u32[]{:S(2)}, u32[]{:S(2)}) collective-permute-start(f32[256]{0:T(256)S(1)} %add.184), channel_id=1, source_target_pairs={{4,0},{5,1},{6,2},{7,3},{8,4},{9,5},{10,6},{11,7},{12,8},{13,9},{1... | collective-permute-start | bytes 3080 | tf_op jit(solution)/shard_map/ppermute | solution.py:192
  227.8 102.6 %collective-permute-start.9 = (f32[256,256]{1,0:T(8,128)S(1)}, f32[256,256]{1,0:T(8,128)S(1)}, u32[]{:S(2)}, u32[]{:S(2)}) collective-permute-start(f32[256,256]{1,0:T(8,128)S(1)} %convolution_add_fusion.2), channel_id=1, source_target_pairs={{4,0},{5,1},{6,2},{7,3},{8,4},{9,5},{10,6},{11,7},{12,8},{13,9},{1... | collective-permute-start | bytes 786440 | tf_op jit(solution)/shard_map/ppermute | solution.py:192
  230.2 103.1 %collective-permute-start.2 = (f32[256,256]{1,0:T(8,128)S(1)}, f32[256,256]{1,0:T(8,128)S(1)}, u32[]{:S(2)}, u32[]{:S(2)}) collective-permute-start(f32[256,256]{1,0:T(8,128)S(1)} %fusion.60), channel_id=1, source_target_pairs={{4,0},{5,1},{6,2},{7,3},{8,4},{9,5},{10,6},{11,7},{12,8},{13,9},{1... | collective-permute-start | bytes 786440 | tf_op jit(solution)/shard_map/ppermute | solution.py:192
  321.7 156.9 %collective-permute-start.6 = (f32[256]{0:T(256)S(1)}, f32[256]{0:T(256)S(1)}, u32[]{:S(2)}, u32[]{:S(2)}) collective-permute-start(f32[256]{0:T(256)S(1)} %add.185), channel_id=1, source_target_pairs={{8,0},{9,1},{10,2},{11,3},{12,4},{13,5},{14,6},{15,7},{24,16},{25,... | collective-permute-start | bytes 3080 | tf_op jit(solution)/shard_map/ppermute | solution.py:192
  331.3 165.3 %collective-permute-start.10 = (f32[256,256]{1,0:T(8,128)S(1)}, f32[256,256]{1,0:T(8,128)S(1)}, u32[]{:S(2)}, u32[]{:S(2)}) collective-permute-start(f32[256,256]{1,0:T(8,128)S(1)} %convolution_add_fusion.1), channel_id=1, source_target_pairs={{8,0},{9,1},{10,2},{11,3},{12,4},{13,5},{14,6},{15,7},{24,16},{25,... | collective-permute-start | bytes 786440 | tf_op jit(solution)/shard_map/ppermute | solution.py:192
where the time goes:
time: 505 us; the launch traced here: 498 us
  waiting for transfers between devices  336 us (67%)
  other arithmetic  100 us (20%)
  blocking collectives  23.1 us (5%)
  starting transfers between devices  16.2 us (3%)
  matrix products  12.2 us (2%)
  local copies, waits for them, and re-layouts  6.42 us (1%)
    ppermute x11, waiting for transfers between devices, shards(): received = lax.ppermute(running, 'tm', pairs)  336 us
    another operation x6, other arithmetic, smoother_elements(): factor = jnp.linalg.cholesky(predicted)  34 us
    another operation x6, other arithmetic, kalman_update(): factor = jnp.linalg.cholesky(normal)  24.9 us
    all_gather x1, blocking collectives, shards(): gathered = lax.all_gather(packed, 'tm', tiled=True)  23.1 us
    another operation x4, other arithmetic, kalman_update(): half = lax.linalg.triangular_solve(factor, rhs, left_side=True, lower=True)  20.9 us
    another operation x3, other arithmetic, smoother_elements(): lax.linalg.triangular_solve(factor, half_solve, left_side=True, lower=Tru...  19.7 us
    ppermute x11, starting transfers between devices, shards(): received = lax.ppermute(running, 'tm', pairs)  16.2 us
  transfers between devices with their start and end apart: 11, of which 9 were waited for; matrix products, arithmetic and copies ran while one was open for 1% of the time, Pallas kernels for 0%

commit v1 on v0

--- a/solution.py
+++ b/solution.py
@@ -118,7 +118,21 @@
     total_steps = tm_count * local_steps
     root_local = jnp.sqrt(obs_masks.astype(jnp.float32) / noise_var)
     packed = jnp.stack([observed, root_local], axis=1)
-    gathered = lax.all_gather(packed, "tm", tiled=True)
+    ways, here, step_2 = (lax.axis_size("tm"), lax.axis_index("tm"), packed.shape[0])
+    lengths = [n * ways if d == 0 else n for d, n in enumerate(packed.shape)]
+    full = lax.dynamic_update_slice_in_dim(
+        jnp.zeros(lengths, packed.dtype), packed, here * step_2, axis=0
+    )
+    going_up = going_down = packed
+    for far in range(1, ways // 2 + 1):
+        going_up = lax.ppermute(going_up, "tm", [(d, (d + 1) % ways) for d in range(ways)])
+        full = lax.dynamic_update_slice_in_dim(full, going_up, (here - far) % ways * step_2, axis=0)
+        if 2 * far < ways:
+            going_down = lax.ppermute(going_down, "tm", [(d, (d - 1) % ways) for d in range(ways)])
+            full = lax.dynamic_update_slice_in_dim(
+                full, going_down, (here + far) % ways * step_2, axis=0
+            )
+    gathered = full
     obs_all = gathered[:, 0]
     root_all = gathered[:, 1]
     mean_first, cov_first = kalman_update(

time: 505 us -> 524 us (1.038)
  starting transfers between devices: 16.2 us -> 46.6 us
  blocking collectives: 23.1 us -> 0 us
  waiting for transfers between devices: 336 us -> 346 us
    ppermute x0 -> x15, starting transfers between devices: none -> 30.4 us  [the longest x7 24.2 us: shards(): lax.ppermute(going_down, 'tm', [(d, (d - 1) % ways) for d in range(ways)])]
    all_gather x1 -> x0, blocking collectives: 23.1 us -> none  [shards(): gathered = lax.all_gather(packed, 'tm', tiled=True)]
    ppermute x0 -> x15, waiting for transfers between devices: none -> 9.78 us  [the longest x8 8.11 us: shards(): lax.ppermute(going_up, 'tm', [(d, (d + 1) % ways) for d in range(ways)])]
  transfers between devices with their start and end apart: 11 -> 26, of which waited for: 9 -> 23; matrix products, arithmetic and copies ran while one was open for 1% -> 1% of each run, Pallas kernels for 0% -> 0%
where the time goes in v1:
time: 524 us; the launch traced here: 517 us
  waiting for transfers between devices  346 us (66%)
  other arithmetic  101 us (19%)
  starting transfers between devices  46.6 us (9%)
  matrix products  12.2 us (2%)
  local copies, waits for them, and re-layouts  7.04 us (1%)
    ppermute x11, waiting for transfers between devices, shards(): received = lax.ppermute(running, 'tm', pairs)  336 us
    another operation x6, other arithmetic, smoother_elements(): factor = jnp.linalg.cholesky(predicted)  34 us
    another operation x6, other arithmetic, kalman_update(): factor = jnp.linalg.cholesky(normal)  24.8 us
    ppermute x7, starting transfers between devices, shards(): lax.ppermute(going_down, 'tm', [(d, (d - 1) % ways) for d in range(ways)])  24.2 us
    another operation x4, other arithmetic, kalman_update(): half = lax.linalg.triangular_solve(factor, rhs, left_side=True, lower=True)  20.9 us
    another operation x3, other arithmetic, smoother_elements(): lax.linalg.triangular_solve(factor, half_solve, left_side=True, lower=Tru...  19.7 us
    ppermute x11, starting transfers between devices, shards(): received = lax.ppermute(running, 'tm', pairs)  16.2 us
  transfers between devices with their start and end apart: 26, of which 23 were waited for; matrix products, arithmetic and copies ran while one was open for 1% of the time, Pallas kernels for 0%

profile of v1, /device:TPU:1, one launch (start us, length us, event | category | flops | bytes accessed | tf_op | source)
XLA Modules:
  0.0 516.9 jit_solution(4608126561545654178)
XLA Ops:
  2.0 2.6 collective-permute-start
  5.3 2.3 collective-permute-start.2
  10.9 3.6 collective-permute-start.5
  15.4 4.9 collective-permute-start.7
  21.0 4.9 collective-permute-start.9
  26.7 5.0 collective-permute-start.11
  32.5 4.9 collective-permute-start.13
  38.3 5.2 %collective-permute-done.14 = f32[1,2,128]{2,1,0:T(2,128)S(1)} collective-permute-done((f32[1,2,128]{2,1,0:T(2,128)S(1)}, f32[1,2,128]{2,1,0:T(2,128)S(1)}, u32[]{:S(2)}, u32[]{:S(2)}) %collective-permute-start.14) | collective-permute-done | bytes 1056 | tf_op jit(solution)/shard_map/ppermute | solution.py:128
  44.0 11.7 %custom-call.32 = f32[128,128]{1,0:T(8,128)S(1)} custom-call(f32[128,128]{1,0:T(8,128)S(1)} %fusion.49), custom_call_target="Cholesky" | custom-call | tf_op jit(solution)/shard_map/jit(cholesky)/cholesky/custom-call.1 | solution.py:77
  57.1 9.8 %custom-call.33 = f32[1,128,128]{1,2,0:T(8,128)S(1)} custom-call(f32[1,128,128]{2,1,0:T(8,128)S(1)} %fusion.47), custom_call_target="InvertDiagBlocksLowerTriangular" | custom-call | tf_op jit(solution)/shard_map/triangular_solve/custom-call.0 | solution.py:80
  68.2 24.9 %while.14 = (s32[]{:T(128)}, f32[256]{0:T(256)S(1)}, f32[256,256]{0,1:T(8,128)S(1)}, s32[]{:T(128)}, f32[128]{0:T(128)S(1)}, /*index=5*/f32[128]{0:T(128)S(1)}, ...) while((s32[]{:T(128)}, f32[256]{0:T(256)S(1)}, ...), condition=%wide.region_3.6_spmd, body=%wide.region_2.5_spmd.sunk | while | flops 152618752 | bytes 5461689 | solution.py:154
  69.2 11.7 %custom-call.37 = f32[128,128]{1,0:T(8,128)S(1)} custom-call(f32[128,128]{1,0:T(8,128)S(1)} %fusion.128), custom_call_target="Cholesky" | custom-call | tf_op jit(solution)/shard_map/while/body/jit(cholesky)/cholesky/custom-call.1 | solution.py:77
  82.2 9.8 %custom-call.38 = f32[1,128,128]{1,2,0:T(8,128)S(1)} custom-call(f32[1,128,128]{2,1,0:T(8,128)S(1)} %fusion.129), custom_call_target="InvertDiagBlocksLowerTriangular" | custom-call | tf_op jit(solution)/shard_map/while/body/triangular_solve/custom-call.0 | solution.py:80
  93.1 63.9 %conditional.1 = (f32[1,256]{1,0:T(1,128)S(1)}, f32[256,256]{0,1:T(8,128)S(1)}, f32[1,256,256]{2,1,0:T(8,128)S(1)}) conditional(s32[]{:T(128)} %convert_element_type.18, (f32[128]{0:T(128)S(1)}, f32[1,256,256]{1,2,0:T(8,128)S(1)}, f32[128]{0:T(128)S(1)}, f32[128]{0:T(128)S(1)}, f32[128]{0:T(128)S(1)}, /*index=5*/f32[256,256]{0,1:T(8,128)S(1)}, ...), branch_computations={%region_4.11_spmd, %region_9.12_spmd} | conditional | flops 556025344 | bytes 11482373 | solution.py:182
  94.2 11.7 %custom-call.24 = f32[1,128,128]{2,1,0:T(8,128)S(1)} custom-call(f32[1,128,128]{2,1,0:T(8,128)S(1)} %cholesky.48), custom_call_target="Cholesky" | custom-call | tf_op jit(solution)/shard_map/cond/branch_0_fun/jit(cholesky)/cholesky | solution.py:90
  106.0 9.8 %custom-call.25 = f32[1,1,128,128]{2,3,1,0:T(8,128)S(1)} custom-call(f32[1,1,128,128]{3,2,1,0:T(8,128)S(1)} %get-tuple-element.207), custom_call_target="InvertDiagBlocksLowerTriangular" | custom-call | tf_op jit(solution)/shard_map/cond/branch_0_fun/jit(cholesky)/cholesky | solution.py:90
  116.3 11.7 %custom-call.26 = f32[1,128,128]{2,1,0:T(8,128)S(1)} custom-call(f32[1,128,128]{2,1,0:T(8,128)S(1)} %fusion.20), custom_call_target="Cholesky" | custom-call | tf_op jit(solution)/shard_map/cond/branch_0_fun/jit(cholesky)/cholesky | solution.py:90
  130.1 4.1 while.13
  130.8 1.3 bitcast_dynamic-update-slice_fusion.3
  134.2 19.7 %custom-call.27 = f32[1,2,128,128]{2,3,1,0:T(8,128)S(1)} custom-call(f32[1,2,128,128]{3,2,1,0:T(8,128)S(1)} %bitcast.294), custom_call_target="InvertDiagBlocksLowerTriangular" | custom-call | tf_op jit(solution)/shard_map/cond/branch_0_fun/triangular_solve | solution.py:92
  157.0 1.9 collective-permute-start.22
  158.9 1.9 collective-permute-start.18
  160.8 1.9 collective-permute-start.15
  162.8 22.1 %collective-permute-done.18 = f32[256]{0:T(256)S(1)} collective-permute-done((f32[256]{0:T(256)S(1)}, f32[256]{0:T(256)S(1)}, u32[]{:S(2)}, u32[]{:S(2)}) %collective-permute-start.18) | collective-permute-done | bytes 1056 | tf_op jit(solution)/shard_map/ppermute | solution.py:206
  190.7 42.7 %collective-permute-done.19 = f32[256]{0:T(256)S(1)} collective-permute-done((f32[256]{0:T(256)S(1)}, f32[256]{0:T(256)S(1)}, u32[]{:S(2)}, u32[]{:S(2)}) %collective-permute-start.19) | collective-permute-done | bytes 1056 | tf_op jit(solution)/shard_map/ppermute | solution.py:206
  233.7 1.3 collective-permute-start.20
  235.0 4.1 collective-permute-done.23
  243.6 92.7 %collective-permute-done.20 = f32[256]{0:T(256)S(1)} collective-permute-done((f32[256]{0:T(256)S(1)}, f32[256]{0:T(256)S(1)}, u32[]{:S(2)}, u32[]{:S(2)}) %collective-permute-start.20) | collective-permute-done | bytes 1056 | tf_op jit(solution)/shard_map/ppermute | solution.py:206
  336.6 1.3 collective-permute-start.21
  337.9 7.4 %collective-permute-done.24 = f32[256,256]{1,0:T(8,128)S(1)} collective-permute-done((f32[256,256]{1,0:T(8,128)S(1)}, f32[256,256]{1,0:T(8,128)S(1)}, u32[]{:S(2)}, u32[]{:S(2)}) %collective-permute-start.24) | collective-permute-done | bytes 262176 | tf_op jit(solution)/shard_map/ppermute | solution.py:206
  348.5 148.8 %collective-permute-done.21 = f32[256]{0:T(256)S(1)} collective-permute-done((f32[256]{0:T(256)S(1)}, f32[256]{0:T(256)S(1)}, u32[]{:S(2)}, u32[]{:S(2)}) %collective-permute-start.21) | collective-permute-done | bytes 1056 | tf_op jit(solution)/shard_map/ppermute | solution.py:206
  498.2 17.0 %collective-permute-done.25 = f32[256,256]{1,0:T(8,128)S(1)} collective-permute-done((f32[256,256]{1,0:T(8,128)S(1)}, f32[256,256]{1,0:T(8,128)S(1)}, u32[]{:S(2)}, u32[]{:S(2)}) %collective-permute-start.25) | collective-permute-done | bytes 262176 | tf_op jit(solution)/shard_map/ppermute | solution.py:206
  (149 shorter events, 38.8 us)
Async XLA Ops:
  1.3 0.7 copy-start.1
  2.0 3.4 collective-permute-start
  4.6 3.3 collective-permute-start.1
  4.6 0.7 copy-start.2
  5.3 4.0 collective-permute-start.2
  7.6 18.8 %copy-start = (f32[128,128]{1,0:T(8,128)S(1)}, f32[128,128]{1,0:T(8,128)}, u32[]{:S(2)}) copy-start(f32[128,128]{1,0:T(8,128)} %param.16) | copy-start | bytes 196612
  7.9 3.0 collective-permute-start.3
  9.4 5.7 %collective-permute-start.4 = (f32[1,2,128]{2,1,0:T(2,128)S(1)}, f32[1,2,128]{2,1,0:T(2,128)S(1)}, u32[]{:S(2)}, u32[]{:S(2)}) collective-permute-start(f32[1,2,128]{2,1,0:T(2,128)S(1)} %collective-permute-done.2), channel_id=1, source_target_pairs={{0,1},{1,2},{2,3},{3,4},{4,5},{5,6},{6,7},{7,8},{8,9},{9,10},{10,1... | collective-permute-start | bytes 3080 | tf_op jit(solution)/shard_map/ppermute | solution.py:128
  10.9 4.5 collective-permute-start.5
  15.1 5.7 %collective-permute-start.6 = (f32[1,2,128]{2,1,0:T(2,128)S(1)}, f32[1,2,128]{2,1,0:T(2,128)S(1)}, u32[]{:S(2)}, u32[]{:S(2)}) collective-permute-start(f32[1,2,128]{2,1,0:T(2,128)S(1)} %collective-permute-done.4), channel_id=1, source_target_pairs={{0,1},{1,2},{2,3},{3,4},{4,5},{5,6},{6,7},{7,8},{8,9},{9,10},{10,1... | collective-permute-start | bytes 3080 | tf_op jit(solution)/shard_map/ppermute | solution.py:128
  15.4 5.7 %collective-permute-start.7 = (f32[1,2,128]{2,1,0:T(2,128)S(1)}, f32[1,2,128]{2,1,0:T(2,128)S(1)}, u32[]{:S(2)}, u32[]{:S(2)}) collective-permute-start(f32[1,2,128]{2,1,0:T(2,128)S(1)} %collective-permute-done.5), channel_id=1, source_target_pairs={{0,15},{1,0},{2,1},{3,2},{4,3},{5,4},{6,5},{7,6},{8,7},{9,8},{10,9... | collective-permute-start | bytes 3080 | tf_op jit(solution)/shard_map/ppermute | solution.py:131
  20.8 5.7 %collective-permute-start.8 = (f32[1,2,128]{2,1,0:T(2,128)S(1)}, f32[1,2,128]{2,1,0:T(2,128)S(1)}, u32[]{:S(2)}, u32[]{:S(2)}) collective-permute-start(f32[1,2,128]{2,1,0:T(2,128)S(1)} %collective-permute-done.6), channel_id=1, source_target_pairs={{0,1},{1,2},{2,3},{3,4},{4,5},{5,6},{6,7},{7,8},{8,9},{9,10},{10,1... | collective-permute-start | bytes 3080 | tf_op jit(solution)/shard_map/ppermute | solution.py:128
  21.0 5.7 %collective-permute-start.9 = (f32[1,2,128]{2,1,0:T(2,128)S(1)}, f32[1,2,128]{2,1,0:T(2,128)S(1)}, u32[]{:S(2)}, u32[]{:S(2)}) collective-permute-start(f32[1,2,128]{2,1,0:T(2,128)S(1)} %collective-permute-done.7), channel_id=1, source_target_pairs={{0,15},{1,0},{2,1},{3,2},{4,3},{5,4},{6,5},{7,6},{8,7},{9,8},{10,9... | collective-permute-start | bytes 3080 | tf_op jit(solution)/shard_map/ppermute | solution.py:131
  26.4 5.7 %collective-permute-start.10 = (f32[1,2,128]{2,1,0:T(2,128)S(1)}, f32[1,2,128]{2,1,0:T(2,128)S(1)}, u32[]{:S(2)}, u32[]{:S(2)}) collective-permute-start(f32[1,2,128]{2,1,0:T(2,128)S(1)} %collective-permute-done.8), channel_id=1, source_target_pairs={{0,1},{1,2},{2,3},{3,4},{4,5},{5,6},{6,7},{7,8},{8,9},{9,10},{10,1... | collective-permute-start | bytes 3080 | tf_op jit(solution)/shard_map/ppermute | solution.py:128
  26.7 5.8 %collective-permute-start.11 = (f32[1,2,128]{2,1,0:T(2,128)S(1)}, f32[1,2,128]{2,1,0:T(2,128)S(1)}, u32[]{:S(2)}, u32[]{:S(2)}) collective-permute-start(f32[1,2,128]{2,1,0:T(2,128)S(1)} %collective-permute-done.9), channel_id=1, source_target_pairs={{0,15},{1,0},{2,1},{3,2},{4,3},{5,4},{6,5},{7,6},{8,7},{9,8},{10,9... | collective-permute-start | bytes 3080 | tf_op jit(solution)/shard_map/ppermute | solution.py:131
  32.1 5.7 %collective-permute-start.12 = (f32[1,2,128]{2,1,0:T(2,128)S(1)}, f32[1,2,128]{2,1,0:T(2,128)S(1)}, u32[]{:S(2)}, u32[]{:S(2)}) collective-permute-start(f32[1,2,128]{2,1,0:T(2,128)S(1)} %collective-permute-done.10), channel_id=1, source_target_pairs={{0,1},{1,2},{2,3},{3,4},{4,5},{5,6},{6,7},{7,8},{8,9},{9,10},{10,1... | collective-permute-start | bytes 3080 | tf_op jit(solution)/shard_map/ppermute | solution.py:128
  32.5 5.7 %collective-permute-start.13 = (f32[1,2,128]{2,1,0:T(2,128)S(1)}, f32[1,2,128]{2,1,0:T(2,128)S(1)}, u32[]{:S(2)}, u32[]{:S(2)}) collective-permute-start(f32[1,2,128]{2,1,0:T(2,128)S(1)} %collective-permute-done.11), channel_id=1, source_target_pairs={{0,15},{1,0},{2,1},{3,2},{4,3},{5,4},{6,5},{7,6},{8,7},{9,8},{10,9... | collective-permute-start | bytes 3080 | tf_op jit(solution)/shard_map/ppermute | solution.py:131
  37.8 5.7 %collective-permute-start.14 = (f32[1,2,128]{2,1,0:T(2,128)S(1)}, f32[1,2,128]{2,1,0:T(2,128)S(1)}, u32[]{:S(2)}, u32[]{:S(2)}) collective-permute-start(f32[1,2,128]{2,1,0:T(2,128)S(1)} %collective-permute-done.12), channel_id=1, source_target_pairs={{0,1},{1,2},{2,3},{3,4},{4,5},{5,6},{6,7},{7,8},{8,9},{9,10},{10,1... | collective-permute-start | bytes 3080 | tf_op jit(solution)/shard_map/ppermute | solution.py:128
  157.0 29.5 %collective-permute-start.22 = (f32[256,256]{1,0:T(8,128)S(1)}, f32[256,256]{1,0:T(8,128)S(1)}, u32[]{:S(2)}, u32[]{:S(2)}) collective-permute-start(f32[256,256]{1,0:T(8,128)S(1)} %bitcast.260), channel_id=1, source_target_pairs={{1,0},{2,1},{3,2},{4,3},{5,4},{6,5},{7,6},{8,7},{9,8},{10,9},{11,1... | collective-permute-start | bytes 786440 | tf_op jit(solution)/shard_map/ppermute | solution.py:206
  158.9 26.0 %collective-permute-start.18 = (f32[256]{0:T(256)S(1)}, f32[256]{0:T(256)S(1)}, u32[]{:S(2)}, u32[]{:S(2)}) collective-permute-start(f32[256]{0:T(256)S(1)} %bitcast.271), channel_id=1, source_target_pairs={{1,0},{2,1},{3,2},{4,3},{5,4},{6,5},{7,6},{8,7},{9,8},{10,9},{11,1... | collective-permute-start | bytes 3080 | tf_op jit(solution)/shard_map/ppermute | solution.py:206
  160.8 27.9 %collective-permute-start.15 = (f32[256,256]{0,1:T(8,128)S(1)}, f32[256,256]{0,1:T(8,128)S(1)}, u32[]{:S(2)}, u32[]{:S(2)}) collective-permute-start(f32[256,256]{0,1:T(8,128)S(1)} %get-tuple-element.136), channel_id=1, source_target_pairs={{1,0},{2,1},{3,2},{4,3},{5,4},{6,5},{7,6},{8,7},{9,8},{10,9},{11,1... | collective-permute-start | bytes 786440 | tf_op jit(solution)/shard_map/ppermute | solution.py:206
  185.1 48.3 %collective-permute-start.19 = (f32[256]{0:T(256)S(1)}, f32[256]{0:T(256)S(1)}, u32[]{:S(2)}, u32[]{:S(2)}) collective-permute-start(f32[256]{0:T(256)S(1)} %add.341), channel_id=1, source_target_pairs={{2,0},{3,1},{4,2},{5,3},{6,4},{7,5},{8,6},{9,7},{10,8},{11,9},{12,... | collective-permute-start | bytes 3080 | tf_op jit(solution)/shard_map/ppermute | solution.py:206
  187.4 51.7 %collective-permute-start.23 = (f32[256,256]{1,0:T(8,128)S(1)}, f32[256,256]{1,0:T(8,128)S(1)}, u32[]{:S(2)}, u32[]{:S(2)}) collective-permute-start(f32[256,256]{1,0:T(8,128)S(1)} %convolution_add_fusion.3), channel_id=1, source_target_pairs={{2,0},{3,1},{4,2},{5,3},{6,4},{7,5},{8,6},{9,7},{10,8},{11,9},{12,... | collective-permute-start | bytes 786440 | tf_op jit(solution)/shard_map/ppermute | solution.py:206
  189.4 52.6 %collective-permute-start.16 = (f32[256,256]{1,0:T(8,128)S(1)}, f32[256,256]{1,0:T(8,128)S(1)}, u32[]{:S(2)}, u32[]{:S(2)}) collective-permute-start(f32[256,256]{1,0:T(8,128)S(1)} %fusion.58), channel_id=1, source_target_pairs={{2,0},{3,1},{4,2},{5,3},{6,4},{7,5},{8,6},{9,7},{10,8},{11,9},{12,... | collective-permute-start | bytes 786440 | tf_op jit(solution)/shard_map/ppermute | solution.py:206
  233.7 102.6 %collective-permute-start.20 = (f32[256]{0:T(256)S(1)}, f32[256]{0:T(256)S(1)}, u32[]{:S(2)}, u32[]{:S(2)}) collective-permute-start(f32[256]{0:T(256)S(1)} %add.342), channel_id=1, source_target_pairs={{4,0},{5,1},{6,2},{7,3},{8,4},{9,5},{10,6},{11,7},{12,8},{13,9},{1... | collective-permute-start | bytes 3080 | tf_op jit(solution)/shard_map/ppermute | solution.py:206
  239.9 105.4 %collective-permute-start.24 = (f32[256,256]{1,0:T(8,128)S(1)}, f32[256,256]{1,0:T(8,128)S(1)}, u32[]{:S(2)}, u32[]{:S(2)}) collective-permute-start(f32[256,256]{1,0:T(8,128)S(1)} %convolution_add_fusion.2), channel_id=1, source_target_pairs={{4,0},{5,1},{6,2},{7,3},{8,4},{9,5},{10,6},{11,7},{12,8},{13,9},{1... | collective-permute-start | bytes 786440 | tf_op jit(solution)/shard_map/ppermute | solution.py:206
  242.3 105.8 %collective-permute-start.17 = (f32[256,256]{1,0:T(8,128)S(1)}, f32[256,256]{1,0:T(8,128)S(1)}, u32[]{:S(2)}, u32[]{:S(2)}) collective-permute-start(f32[256,256]{1,0:T(8,128)S(1)} %fusion.59), channel_id=1, source_target_pairs={{4,0},{5,1},{6,2},{7,3},{8,4},{9,5},{10,6},{11,7},{12,8},{13,9},{1... | collective-permute-start | bytes 786440 | tf_op jit(solution)/shard_map/ppermute | solution.py:206
  336.6 160.8 %collective-permute-start.21 = (f32[256]{0:T(256)S(1)}, f32[256]{0:T(256)S(1)}, u32[]{:S(2)}, u32[]{:S(2)}) collective-permute-start(f32[256]{0:T(256)S(1)} %add.343), channel_id=1, source_target_pairs={{8,0},{9,1},{10,2},{11,3},{12,4},{13,5},{14,6},{15,7},{24,16},{25,... | collective-permute-start | bytes 3080 | tf_op jit(solution)/shard_map/ppermute | solution.py:206
  346.1 169.1 %collective-permute-start.25 = (f32[256,256]{1,0:T(8,128)S(1)}, f32[256,256]{1,0:T(8,128)S(1)}, u32[]{:S(2)}, u32[]{:S(2)}) collective-permute-start(f32[256,256]{1,0:T(8,128)S(1)} %convolution_add_fusion.1), channel_id=1, source_target_pairs={{8,0},{9,1},{10,2},{11,3},{12,4},{13,5},{14,6},{15,7},{24,16},{25,... | collective-permute-start | bytes 786440 | tf_op jit(solution)/shard_map/ppermute | solution.py:206
